TPU v7x, 256 devices: a whole 4x4x8 slice. The times are simulated.
256 devices in a mesh: tm: 16 (over z, core), tile: 16 (over x, y).
Axes of the slice: x: 4, y: 4, z: 8, core: 2. Of those that a mesh axis runs over, the one named last changes fastest.
Arguments:
- obs_values: bfloat16 [16, 32768, 128], P('tm', 'tile'), may hold values from -6 to 6
- obs_weight: bfloat16 [16, 32768, 128], P('tm', 'tile'), may hold values from 0.19921875 to 2
- obs_count: int32 [16, 32768], P('tm', 'tile'), may hold values from 32 to 128
- dest_tile: int32 [16, 32768, 1], P('tm', 'tile'), may hold values from 0 to 15; in each aligned block of 2048 rows (0 to 2047, 2048 to 4095, ..., all dimensions but the last counted through in order) at most 256 rows name the same one
- jac_index: int32 [16, 32768], P('tm', 'tile'), may hold values from 0 to 255
- jacobian: bfloat16 [16, 4096, 128, 128], P('tm', 'tile'), may hold values from -0.5 to 0.5
- jac_state: int32 [16, 4096], P('tm', 'tile'), may hold values from 0 to 63
- corr_blocks: bfloat16 [16, 768, 128, 128], P('tm', 'tile'), may hold values from -0.625 to 0.625
- corr_row: int32 [16, 768], P('tm', 'tile'), may hold values from 0 to 63
- corr_col: int32 [16, 768], P('tm', 'tile'), may hold values from 0 to 63
- time_coupling: bfloat16 [16, 1024, 128], P('tm', 'tile'), may hold values from 0.19921875 to 0.59765625
Outputs:
- product: bfloat16 [16, 32768, 128], P('tm', 'tile')
Inputs may be any that keep to these rules, and one draw needn't show every extreme that they name: `dest_tile`: in the rows of one device, no tile is named by more than 256 observation blocks, a bound that some block reaches.
All inputs are finite; a program needn't handle non-finite values.
Results may differ from a plain program's by a relative error of at most 0.0075.
Values may be sent and summed in bfloat16 or wider, within the bound.
No kernel may reach another device: no remote copies, remote signals or barrier semaphores. Data moves between devices by JAX's collectives and lax.ppermute only.
A program may use at most 64 MiB of HBM per device.

v0:
```python
import jax
import jax.numpy as jnp
from jax import lax
from jax.sharding import PartitionSpec as P


def from_behind(x, axis, by):
    length = lax.axis_size(axis)
    pairs = [(i, i + by) for i in range(length) if 0 <= i + by < length]
    return lax.ppermute(x, axis, pairs)


def shards(
    obs_values,
    obs_weight,
    obs_count,
    dest_tile,
    jac_index,
    jacobian,
    jac_state,
    corr_blocks,
    corr_row,
    corr_col,
    time_coupling,
):
    obs_total = obs_values.shape[1]
    block_width = obs_values.shape[2]
    jac_total = jacobian.shape[1]
    state_total = time_coupling.shape[1]
    lane_index = lax.broadcasted_iota(jnp.int32, (obs_total, block_width), 1)
    keeping = (lane_index < obs_count[0][:, None]).astype(jnp.float32)
    weighted = (
        obs_values[0].astype(jnp.float32) * obs_weight[0].astype(jnp.float32) * keeping
    ).astype(jnp.bfloat16)
    target = dest_tile[0, :, 0]
    column = jac_index[0]
    bin_id = target * jac_total + column
    row_ids = lax.broadcasted_iota(jnp.int32, (jac_total * lax.axis_size("tile"), obs_total), 0)
    picker = (row_ids == bin_id[None, :]).astype(jnp.bfloat16)
    summed = lax.psum_scatter(
        jnp.dot(picker, weighted, preferred_element_type=jnp.float32),
        "tile",
        scatter_dimension=0,
        tiled=True,
    )
    merged = summed.astype(jnp.bfloat16)
    spread = jnp.einsum("kij,ki->kj", jacobian[0], merged, preferred_element_type=jnp.float32)
    state_ids = lax.broadcasted_iota(jnp.int32, (state_total, jac_total), 0)
    owners = state_ids == jac_state[0][None, :]
    state = jnp.dot(owners.astype(jnp.float32), spread, precision=lax.Precision.HIGHEST).astype(
        jnp.bfloat16
    )
    corr_total = corr_blocks.shape[1]
    read_ids = lax.broadcasted_iota(jnp.int32, (corr_total, state_total), 1)
    reader = (read_ids == corr_col[0][:, None]).astype(jnp.bfloat16)
    source = jnp.dot(reader, state, preferred_element_type=jnp.float32).astype(jnp.bfloat16)
    mixing = jnp.einsum("cij,cj->ci", corr_blocks[0], source, preferred_element_type=jnp.float32)
    write_ids = lax.broadcasted_iota(jnp.int32, (state_total, corr_total), 0)
    writer = (write_ids == corr_row[0][None, :]).astype(jnp.float32)
    spatial = jnp.dot(writer, mixing, precision=lax.Precision.HIGHEST).astype(jnp.bfloat16)
    coupling = time_coupling[0]
    earlier = from_behind(spatial, "tm", 1)
    later_state, later_coupling = from_behind((spatial, coupling), "tm", -1)
    coupled = (
        spatial.astype(jnp.float32)
        + coupling.astype(jnp.float32) * earlier.astype(jnp.float32)
        + later_coupling.astype(jnp.float32) * later_state.astype(jnp.float32)
    ).astype(jnp.bfloat16)
    local_state = jnp.dot(
        owners.T.astype(jnp.bfloat16), coupled, preferred_element_type=jnp.float32
    ).astype(jnp.bfloat16)
    model_obs = jnp.einsum(
        "kij,kj->ki", jacobian[0], local_state, preferred_element_type=jnp.float32
    ).astype(jnp.bfloat16)
    portion = lax.all_gather(model_obs, "tile", axis=0, tiled=True)
    columns = lax.broadcasted_iota(jnp.int32, (obs_total, portion.shape[0]), 1)
    picker = (bin_id[:, None] == columns).astype(jnp.bfloat16)
    gathered = jnp.dot(picker, portion, preferred_element_type=jnp.float32)
    return (gathered * keeping).astype(jnp.bfloat16)[None]


def solution(mesh):
    in_specs = (
        P("tm", "tile", None),
        P("tm", "tile", None),
        P("tm", "tile"),
        P("tm", "tile", None),
        P("tm", "tile"),
        P("tm", "tile", None, None),
        P("tm", "tile"),
        P("tm", "tile", None, None),
        P("tm", "tile"),
        P("tm", "tile"),
        P("tm", "tile", None),
    )
    out_specs = P("tm", "tile", None)
    return jax.shard_map(shards, mesh=mesh, in_specs=in_specs, out_specs=out_specs, check_vma=False)
```

profile of v0, /device:TPU:2, one launch (start us, length us, event | category | flops | bytes accessed | tf_op | source)
XLA Modules:
  0.0 185.7 jit_solution(13283383729035749452)
XLA Ops:
  6.5 0.0 copy-start
  6.5 0.0 reduce-scatter.2.cloned.1.call-start
  6.5 0.8 bitcast_add_fusion
  7.4 0.0 copy-start.3
  7.4 8.6 %fusion = f32[4096,128]{1,0:T(8,128)} fusion(s32[2048]{0:T(1024)S(1)} %bitcast.51, bf16[1,2048,128]{2,1,0:T(8,128)(2,1)} %param.12, bf16[1,2048,128]{2,1,0:T(8,128)(2,1)} %param.11, s32[2048]{0:T(1024)} %bitcast.55), kind=kOutput, calls=%fused_computation.2 | convolution fusion | flops 2157445120 | bytes 3162112 | tf_op jit(solution)/shard_map/dot_general | solution.py:41
  16.0 0.0 reduce-scatter.2.cloned.1.call-update
  16.0 0.0 all-gather.2.cloned.1.call-start
  16.1 0.0 copy-done.3
  16.1 1.3 collective-permute-start.1
  17.4 81.6 %reduce-scatter.2.cloned.1.call-done = f32[256,128]{1,0:T(8,128)} async-done(((f32[4096,128]{1,0:T(8,128)}), f32[256,128]{1,0:T(8,128)}) %reduce-scatter.2.cloned.1.call-update) | async-done | bytes 131088 | tf_op jit(solution)/shard_map/reduce_scatter | solution.py:40
  99.0 0.9 convert_bitcast_fusion
  99.9 0.0 copy-start.1
  99.9 0.0 copy-start.6
  99.9 5.7 %fusion.6 = f32[256,1,128]{2,1,0:T(1,128)S(1)} fusion(bf16[1,256,128,128]{3,2,1,0:T(8,128)(2,1)} %param.16, bf16[256,128,1]{1,0,2:T(8,128)(2,1)S(1)} %convert_bitcast_fusion), kind=kOutput, calls=%fused_computation.8 | convolution fusion | flops 8388608 | bytes 8585216 | tf_op jit(solution)/shard_map/kij,ki->kj/dot_general | solution.py:47
  105.6 0.0 copy-done.4
  105.6 0.2 convolution_convert_fusion.2
  105.8 0.0 copy-done.7
  105.8 0.2 fusion.14
  106.0 0.0 copy-done
  106.0 0.9 fusion.11
  106.9 0.2 convolution_convert_fusion.1
  107.1 1.3 collective-permute-start
  108.4 1.5 collective-permute-start.2
  109.9 0.0 collective-permute-done.1
  109.9 0.0 collective-permute-done
  109.9 3.4 %collective-permute-done.2 = bf16[64,128]{1,0:T(8,128)(2,1)S(1)} collective-permute-done((bf16[64,128]{1,0:T(8,128)(2,1)S(1)}, bf16[64,128]{1,0:T(8,128)(2,1)S(1)}, u32[]{:S(2)}, u32[]{:S(2)}) %collective-permute-start.2) | collective-permute-done | bytes 16416 | tf_op jit(solution)/shard_map/ppermute | solution.py:10
  113.3 0.2 fusion.13
  113.5 7.8 %fusion.4 = f32[256,1,128]{2,1,0:T(1,128)S(1)} fusion(bf16[1,256,128,128]{3,2,1,0:T(8,128)(2,1)} %param.16, bf16[256,128,1]{1,0,2:T(8,128)(2,1)S(1)} %fusion.13), kind=kOutput, calls=%fused_computation.6 | convolution fusion | flops 8388608 | bytes 8585216 | tf_op jit(solution)/shard_map/kij,kj->ki/dot_general | solution.py:72
  121.3 0.7 convert_element_type.71
  121.9 0.0 all-gather.2.cloned.1.call-update
  122.0 49.3 %all-gather.2.cloned.1.call-done = bf16[4096,128]{1,0:T(8,128)(2,1)} async-done(((bf16[256,128]{1,0:T(8,128)(2,1)}), bf16[4096,128]{1,0:T(8,128)(2,1)}) %all-gather.2.cloned.1.call-update) | async-done | bytes 1048592 | tf_op jit(solution)/shard_map/all_gather | solution.py:75
  171.3 7.6 %fusion.10 = bf16[1,2048,128]{2,1,0:T(8,128)(2,1)} fusion(bf16[4096,128]{1,0:T(8,128)(2,1)} %all-gather.2.cloned.1.call-done, s32[2048]{0:T(1024)S(1)} %add.18, s32[2048]{0:T(1024)S(1)} %bitcast.56), kind=kOutput, calls=%fused_computation.12 | convolution fusion | flops 2156658688 | bytes 1589248 | tf_op jit(solution)/shard_map/dot_general | solution.py:78
  (10 shorter events, 0.0 us)
Async XLA Ops:
  6.5 99.5 %copy-start = (bf16[1,48,128,128]{3,2,1,0:T(8,128)(2,1)S(1)}, bf16[1,48,128,128]{3,2,1,0:T(8,128)(2,1)}, u32[]{:S(2)}) copy-start(bf16[1,48,128,128]{3,2,1,0:T(8,128)(2,1)} %param.18) | copy-start | bytes 4718596
  6.5 92.5 %reduce-scatter.2.cloned.1.call-start = ((), (), s32[]{:S(2)}) async-start(), calls=%async_computation.1 | async-start | bytes 2228224 | tf_op jit(solution)/shard_map/reduce_scatter | solution.py:40
  7.4 8.7 %copy-start.3 = (bf16[1,64,128]{2,1,0:T(8,128)(2,1)S(1)}, bf16[1,64,128]{2,1,0:T(8,128)(2,1)}, u32[]{:S(2)}) copy-start(bf16[1,64,128]{2,1,0:T(8,128)(2,1)} %param.21) | copy-start | bytes 49156
  16.0 89.6 %copy-start.4 = (s32[1,256]{1,0:T(1,128)S(1)}, s32[1,256]{1,0:T(1,128)}, u32[]{:S(2)}) copy-start(s32[1,256]{1,0:T(1,128)} %param.17) | copy-start | bytes 3076
  16.0 89.8 %copy-start.7 = (s32[1,48]{1,0:T(1,128)S(1)}, s32[1,48]{1,0:T(1,128)}, u32[]{:S(2)}) copy-start(s32[1,48]{1,0:T(1,128)} %param.20) | copy-start | bytes 580
  16.0 90.9 %copy-start.5 = (s32[1,48]{1,0:T(1,128)S(1)}, s32[1,48]{1,0:T(1,128)}, u32[]{:S(2)}) copy-start(s32[1,48]{1,0:T(1,128)} %param.19) | copy-start | bytes 580
  16.0 155.3 %all-gather.2.cloned.1.call-start = ((), (), s32[]{:S(2)}) async-start(), calls=%async_computation.2 | async-start | bytes 1114112 | tf_op jit(solution)/shard_map/all_gather | solution.py:75
  16.1 93.8 %collective-permute-start.1 = (bf16[64,128]{1,0:T(8,128)(2,1)S(1)}, bf16[64,128]{1,0:T(8,128)(2,1)S(1)}, u32[]{:S(2)}, u32[]{:S(2)}) collective-permute-start(bf16[64,128]{1,0:T(8,128)(2,1)S(1)} %bitcast.50), channel_id=1, source_target_pairs={{16,0},{32,16},{48,32},{64,48},{80,64},{96,80},{112,96},{128,112},... | collective-permute-start | bytes 49160 | tf_op jit(solution)/shard_map/ppermute | solution.py:10
  99.9 22.0 %copy-start.2 = (s32[1,2048,1]{1,2,0:T(1,128)S(1)}, s32[1,2048,1]{1,2,0:T(1,128)}, u32[]{:S(2)}) copy-start(s32[1,2048,1]{1,2,0:T(1,128)} %param.14) | copy-start | bytes 24580
  99.9 22.1 %copy-start.1 = (s32[1,2048]{1,0:T(1,128)S(1)}, s32[1,2048]{1,0:T(1,128)}, u32[]{:S(2)}) copy-start(s32[1,2048]{1,0:T(1,128)} %param.15) | copy-start | bytes 24580
  99.9 71.4 %copy-start.6 = (s32[1,2048]{1,0:T(1,128)S(1)}, s32[1,2048]{1,0:T(1,128)}, u32[]{:S(2)}) copy-start(s32[1,2048]{1,0:T(1,128)} %param.13) | copy-start | bytes 24580
  107.1 2.8 %collective-permute-start = (bf16[64,128]{1,0:T(8,128)(2,1)S(1)}, bf16[64,128]{1,0:T(8,128)(2,1)S(1)}, u32[]{:S(2)}, u32[]{:S(2)}) collective-permute-start(bf16[64,128]{1,0:T(8,128)(2,1)S(1)} %convolution_convert_fusion.1), channel_id=1, source_target_pairs={{0,16},{16,32},{32,48},{48,64},{64,80},{80,96},{96,112},{112,128},... | collective-permute-start | bytes 49160 | tf_op jit(solution)/shard_map/ppermute | solution.py:10
  108.4 4.9 %collective-permute-start.2 = (bf16[64,128]{1,0:T(8,128)(2,1)S(1)}, bf16[64,128]{1,0:T(8,128)(2,1)S(1)}, u32[]{:S(2)}, u32[]{:S(2)}) collective-permute-start(bf16[64,128]{1,0:T(8,128)(2,1)S(1)} %convolution_convert_fusion.1), channel_id=1, source_target_pairs={{16,0},{32,16},{48,32},{64,48},{80,64},{96,80},{112,96},{128,112},... | collective-permute-start | bytes 49160 | tf_op jit(solution)/shard_map/ppermute | solution.py:10
Sparse Core Ops, SparseCore 0:
  16.1 82.8 reduce-scatter.1
  122.1 49.1 all-gather.1
where the time goes:
time: 186 us
  waiting for transfers between devices  134 us (72%)
  matrix products  31.3 us (17%)
  between operations  13.5 us (7%)
  starting transfers between devices  4.1 us (2%)
  other arithmetic  2.44 us (1%)
    reduce_scatter x1, waiting for transfers between devices, shards(): lax.psum_scatter(jnp.dot(picker, weighted, preferred_element_type=jnp.flo...  81.6 us
    all_gather x1, waiting for transfers between devices, shards(): portion = lax.all_gather(model_obs, 'tile', axis=0, tiled=True)  49.3 us
    dot_general x1, matrix products, shards(): jnp.dot(picker, weighted, preferred_element_type=jnp.float32)  8.59 us
    dot_general x1, matrix products, shards(): jnp.einsum('kij,kj->ki', jacobian[0], local_state, preferred_element_type...  7.78 us
    dot_general x1, matrix products, shards(): gathered = jnp.dot(picker, portion, preferred_element_type=jnp.float32)  7.57 us
    dot_general x1, matrix products, shards(): jnp.einsum('kij,ki->kj', jacobian[0], merged, preferred_element_type=jnp....  5.66 us
    ppermute x3, starting transfers between devices, from_behind(): return lax.ppermute(x, axis, pairs)  4.06 us
  transfers between devices with their start and end apart: 5, of which 3 were waited for; matrix products, arithmetic and copies ran while one was open for 4% of the time, Pallas kernels for 0%

commit v1 on v0

--- a/solution.py
+++ b/solution.py
@@ -1,7 +1,19 @@
+import functools
 import jax
 import jax.numpy as jnp
 from jax import lax
 from jax.sharding import PartitionSpec as P
+
+
+def lift_fields(mat, axis_tag):
+    built = lax.axis_size(axis_tag)
+    r2 = jnp.stack([mat] * built)
+    local_out = lax.all_to_all(r2, axis_name=axis_tag, split_axis=0, concat_axis=0)
+    response = jnp.concatenate(local_out, axis=0)
+    return response
+
+
+part_panels_in = functools.partial(lift_fields, axis_tag="tile")
 
 
 def from_behind(x, axis, by):
@@ -72,7 +84,7 @@
     model_obs = jnp.einsum(
         "kij,kj->ki", jacobian[0], local_state, preferred_element_type=jnp.float32
     ).astype(jnp.bfloat16)
-    portion = lax.all_gather(model_obs, "tile", axis=0, tiled=True)
+    portion = part_panels_in(model_obs)
     columns = lax.broadcasted_iota(jnp.int32, (obs_total, portion.shape[0]), 1)
     picker = (bin_id[:, None] == columns).astype(jnp.bfloat16)
     gathered = jnp.dot(picker, portion, preferred_element_type=jnp.float32)

time: 186 us -> 162 us (0.87)
  the two profiles are of different devices: /device:TPU:2 before, /device:TPU:1 now
where the time goes in v1:
time: 162 us
  waiting for transfers between devices  97.1 us (60%)
  matrix products  30.7 us (19%)
  starting transfers between devices  17.2 us (11%)
  between operations  13.5 us (8%)
  other arithmetic  1.8 us (1%)
    reduce_scatter x1, waiting for transfers between devices, shards(): lax.psum_scatter(jnp.dot(picker, weighted, preferred_element_type=jnp.flo...  77.2 us
    all_to_all x1, waiting for transfers between devices, lift_fields(): lax.all_to_all(r2, axis_name=axis_tag, split_axis=0, concat_axis=0)  16.8 us
    ppermute x3, starting transfers between devices, from_behind(): return lax.ppermute(x, axis, pairs)  12.6 us
    dot_general x1, matrix products, shards(): jnp.dot(picker, weighted, preferred_element_type=jnp.float32)  8.58 us
    dot_general x1, matrix products, shards(): jnp.einsum('kij,kj->ki', jacobian[0], local_state, preferred_element_type...  7.78 us
    dot_general x1, matrix products, shards(): gathered = jnp.dot(picker, portion, preferred_element_type=jnp.float32)  6.99 us
    dot_general x1, matrix products, shards(): jnp.einsum('kij,ki->kj', jacobian[0], merged, preferred_element_type=jnp....  5.65 us
    all_to_all x1, starting transfers between devices, lift_fields(): lax.all_to_all(r2, axis_name=axis_tag, split_axis=0, concat_axis=0)  4.66 us
  transfers between devices with their start and end apart: 5, of which 3 were waited for; matrix products, arithmetic and copies ran while one was open for 5% of the time, Pallas kernels for 0%

profile of v1, /device:TPU:1, one launch (start us, length us, event | category | flops | bytes accessed | tf_op | source)
XLA Modules:
  0.0 161.5 jit_solution(11691634229986752999)
XLA Ops:
  6.5 0.0 copy-start
  6.5 0.0 reduce-scatter.2.cloned.1.call-start
  6.5 0.8 bitcast_add_fusion
  7.4 0.0 copy-start.3
  7.4 8.6 %fusion = f32[4096,128]{1,0:T(8,128)} fusion(s32[2048]{0:T(1024)S(1)} %bitcast.53, bf16[1,2048,128]{2,1,0:T(8,128)(2,1)} %param.12, bf16[1,2048,128]{2,1,0:T(8,128)(2,1)} %param.11, s32[2048]{0:T(1024)} %bitcast.57), kind=kOutput, calls=%fused_computation.2 | convolution fusion | flops 2157445120 | bytes 3162112 | tf_op jit(solution)/shard_map/dot_general | solution.py:53
  16.0 0.0 reduce-scatter.2.cloned.1.call-update
  16.0 0.0 copy-done.3
  16.0 5.2 %collective-permute-start.1 = (bf16[64,128]{1,0:T(8,128)(2,1)S(1)}, bf16[64,128]{1,0:T(8,128)(2,1)S(1)}, u32[]{:S(2)}, u32[]{:S(2)}) collective-permute-start(bf16[64,128]{1,0:T(8,128)(2,1)S(1)} %bitcast.52), channel_id=1, source_target_pairs={{16,0},{32,16},{48,32},{64,48},{80,64},{96,80},{112,96},{128,112},... | collective-permute-start | bytes 49160 | tf_op jit(solution)/shard_map/ppermute | solution.py:22
  21.3 77.2 %reduce-scatter.2.cloned.1.call-done = f32[256,128]{1,0:T(8,128)} async-done(((f32[4096,128]{1,0:T(8,128)}), f32[256,128]{1,0:T(8,128)}) %reduce-scatter.2.cloned.1.call-update) | async-done | bytes 131088 | tf_op jit(solution)/shard_map/reduce_scatter | solution.py:52
  98.4 0.9 convert_bitcast_fusion
  99.4 5.6 %fusion.6 = f32[256,1,128]{2,1,0:T(1,128)S(1)} fusion(bf16[1,256,128,128]{3,2,1,0:T(8,128)(2,1)} %param.16, bf16[256,128,1]{1,0,2:T(8,128)(2,1)S(1)} %convert_bitcast_fusion), kind=kOutput, calls=%fused_computation.8 | convolution fusion | flops 8388608 | bytes 8585216 | tf_op jit(solution)/shard_map/kij,ki->kj/dot_general | solution.py:59
  105.0 0.0 copy-done.4
  105.0 0.2 convolution_convert_fusion.2
  105.2 0.0 copy-done.7
  105.2 0.2 fusion.14
  105.4 0.0 copy-done
  105.4 0.9 fusion.11
  106.3 0.0 copy-done.5
  106.3 0.2 convolution_convert_fusion.1
  106.5 5.4 %collective-permute-start = (bf16[64,128]{1,0:T(8,128)(2,1)S(1)}, bf16[64,128]{1,0:T(8,128)(2,1)S(1)}, u32[]{:S(2)}, u32[]{:S(2)}) collective-permute-start(bf16[64,128]{1,0:T(8,128)(2,1)S(1)} %convolution_convert_fusion.1), channel_id=1, source_target_pairs={{0,16},{16,32},{32,48},{48,64},{64,80},{80,96},{96,112},{112,128},... | collective-permute-start | bytes 49160 | tf_op jit(solution)/shard_map/ppermute | solution.py:22
  111.9 1.9 %collective-permute-start.2 = (bf16[64,128]{1,0:T(8,128)(2,1)S(1)}, bf16[64,128]{1,0:T(8,128)(2,1)S(1)}, u32[]{:S(2)}, u32[]{:S(2)}) collective-permute-start(bf16[64,128]{1,0:T(8,128)(2,1)S(1)} %convolution_convert_fusion.1), channel_id=1, source_target_pairs={{16,0},{32,16},{48,32},{64,48},{80,64},{96,80},{112,96},{128,112},... | collective-permute-start | bytes 49160 | tf_op jit(solution)/shard_map/ppermute | solution.py:22
  113.8 0.0 collective-permute-done.1
  113.9 0.0 collective-permute-done
  113.9 3.1 %collective-permute-done.2 = bf16[64,128]{1,0:T(8,128)(2,1)S(1)} collective-permute-done((bf16[64,128]{1,0:T(8,128)(2,1)S(1)}, bf16[64,128]{1,0:T(8,128)(2,1)S(1)}, u32[]{:S(2)}, u32[]{:S(2)}) %collective-permute-start.2) | collective-permute-done | bytes 16416 | tf_op jit(solution)/shard_map/ppermute | solution.py:22
  117.0 0.2 fusion.13
  117.2 7.8 %fusion.4 = f32[256,1,128]{2,1,0:T(1,128)S(1)} fusion(bf16[1,256,128,128]{3,2,1,0:T(8,128)(2,1)} %param.16, bf16[256,128,1]{1,0,2:T(8,128)(2,1)S(1)} %fusion.13), kind=kOutput, calls=%fused_computation.6 | convolution fusion | flops 8388608 | bytes 8585216 | tf_op jit(solution)/shard_map/kij,kj->ki/dot_general | solution.py:84
  125.0 1.2 stack.2
  126.2 4.7 %all-to-all-start = ((bf16[16,256,128]{2,1,0:T(8,128)(2,1)}), bf16[16,256,128]{2,1,0:T(8,128)(2,1)S(1)}, u32[]{:S(2)}, u32[]{:S(2)}) async-start(bf16[16,256,128]{2,1,0:T(8,128)(2,1)} %stack.2), calls=%async_computation.1 | async-start | bytes 2097152 | tf_op jit(solution)/shard_map/all_to_all | solution.py:11
  130.9 0.0 copy-done.2
  130.9 0.0 copy-done.1
  130.9 16.8 %all-to-all-done = bf16[16,256,128]{2,1,0:T(8,128)(2,1)S(1)} async-done(((bf16[16,256,128]{2,1,0:T(8,128)(2,1)}), bf16[16,256,128]{2,1,0:T(8,128)(2,1)S(1)}, u32[]{:S(2)}, u32[]{:S(2)}) %all-to-all-start) | async-done | bytes 1048608 | tf_op jit(solution)/shard_map/all_to_all | solution.py:11
  147.7 7.0 %fusion.10 = bf16[1,2048,128]{2,1,0:T(8,128)(2,1)} fusion(bf16[4096,128]{1,0:T(8,128)(2,1)S(1)} %bitcast.46, s32[2048]{0:T(1024)S(1)} %add.18, s32[2048]{0:T(1024)S(1)} %bitcast.58), kind=kOutput, calls=%fused_computation.12 | convolution fusion | flops 2156658688 | bytes 1589248 | tf_op jit(solution)/shard_map/dot_general | solution.py:90
  (10 shorter events, 0.1 us)
Async XLA Ops:
  6.5 98.9 %copy-start = (bf16[1,48,128,128]{3,2,1,0:T(8,128)(2,1)S(1)}, bf16[1,48,128,128]{3,2,1,0:T(8,128)(2,1)}, u32[]{:S(2)}) copy-start(bf16[1,48,128,128]{3,2,1,0:T(8,128)(2,1)} %param.18) | copy-start | bytes 4718596
  6.5 91.9 %reduce-scatter.2.cloned.1.call-start = ((), (), s32[]{:S(2)}) async-start(), calls=%async_computation.2 | async-start | bytes 2228224 | tf_op jit(solution)/shard_map/reduce_scatter | solution.py:52
  7.4 8.6 %copy-start.3 = (bf16[1,64,128]{2,1,0:T(8,128)(2,1)S(1)}, bf16[1,64,128]{2,1,0:T(8,128)(2,1)}, u32[]{:S(2)}) copy-start(bf16[1,64,128]{2,1,0:T(8,128)(2,1)} %param.21) | copy-start | bytes 49156
  16.0 89.0 %copy-start.4 = (s32[1,256]{1,0:T(1,128)S(1)}, s32[1,256]{1,0:T(1,128)}, u32[]{:S(2)}) copy-start(s32[1,256]{1,0:T(1,128)} %param.17) | copy-start | bytes 3076
  16.0 89.2 %copy-start.7 = (s32[1,48]{1,0:T(1,128)S(1)}, s32[1,48]{1,0:T(1,128)}, u32[]{:S(2)}) copy-start(s32[1,48]{1,0:T(1,128)} %param.20) | copy-start | bytes 580
  16.0 90.4 %copy-start.5 = (s32[1,48]{1,0:T(1,128)S(1)}, s32[1,48]{1,0:T(1,128)}, u32[]{:S(2)}) copy-start(s32[1,48]{1,0:T(1,128)} %param.19) | copy-start | bytes 580
  16.0 97.8 %collective-permute-start.1 = (bf16[64,128]{1,0:T(8,128)(2,1)S(1)}, bf16[64,128]{1,0:T(8,128)(2,1)S(1)}, u32[]{:S(2)}, u32[]{:S(2)}) collective-permute-start(bf16[64,128]{1,0:T(8,128)(2,1)S(1)} %bitcast.52), channel_id=1, source_target_pairs={{16,0},{32,16},{48,32},{64,48},{80,64},{96,80},{112,96},{128,112},... | collective-permute-start | bytes 49160 | tf_op jit(solution)/shard_map/ppermute | solution.py:22
  105.0 25.8 %copy-start.2 = (s32[1,2048,1]{1,2,0:T(1,128)S(1)}, s32[1,2048,1]{1,2,0:T(1,128)}, u32[]{:S(2)}) copy-start(s32[1,2048,1]{1,2,0:T(1,128)} %param.14) | copy-start | bytes 24580
  105.0 25.9 %copy-start.1 = (s32[1,2048]{1,0:T(1,128)S(1)}, s32[1,2048]{1,0:T(1,128)}, u32[]{:S(2)}) copy-start(s32[1,2048]{1,0:T(1,128)} %param.15) | copy-start | bytes 24580
  105.0 42.7 %copy-start.6 = (s32[1,2048]{1,0:T(1,128)S(1)}, s32[1,2048]{1,0:T(1,128)}, u32[]{:S(2)}) copy-start(s32[1,2048]{1,0:T(1,128)} %param.13) | copy-start | bytes 24580
  106.5 7.3 %collective-permute-start = (bf16[64,128]{1,0:T(8,128)(2,1)S(1)}, bf16[64,128]{1,0:T(8,128)(2,1)S(1)}, u32[]{:S(2)}, u32[]{:S(2)}) collective-permute-start(bf16[64,128]{1,0:T(8,128)(2,1)S(1)} %convolution_convert_fusion.1), channel_id=1, source_target_pairs={{0,16},{16,32},{32,48},{48,64},{64,80},{80,96},{96,112},{112,128},... | collective-permute-start | bytes 49160 | tf_op jit(solution)/shard_map/ppermute | solution.py:22
  111.9 5.1 %collective-permute-start.2 = (bf16[64,128]{1,0:T(8,128)(2,1)S(1)}, bf16[64,128]{1,0:T(8,128)(2,1)S(1)}, u32[]{:S(2)}, u32[]{:S(2)}) collective-permute-start(bf16[64,128]{1,0:T(8,128)(2,1)S(1)} %convolution_convert_fusion.1), channel_id=1, source_target_pairs={{16,0},{32,16},{48,32},{64,48},{80,64},{96,80},{112,96},{128,112},... | collective-permute-start | bytes 49160 | tf_op jit(solution)/shard_map/ppermute | solution.py:22
  126.2 21.5 %all-to-all-start = ((bf16[16,256,128]{2,1,0:T(8,128)(2,1)}), bf16[16,256,128]{2,1,0:T(8,128)(2,1)S(1)}, u32[]{:S(2)}, u32[]{:S(2)}) async-start(bf16[16,256,128]{2,1,0:T(8,128)(2,1)} %stack.2), calls=%async_computation.1 | async-start | bytes 2097152 | tf_op jit(solution)/shard_map/all_to_all | solution.py:11
Sparse Core Ops, SparseCore 0:
  16.1 82.2 reduce-scatter.1
